TPU v7x, 32 devices: a whole 2x2x4 slice. The times are simulated.
32 devices in a mesh: blk: 8 (over y, x, core), xfer: 4 (over z).
Axes of the slice: x: 2, y: 2, z: 4, core: 2. Of those that a mesh axis runs over, the one named last changes fastest.
Arguments:
- greens: bfloat16 [8, 2, 256, 256], P('blk'), may hold values from -6 to 6
- transfer_index: int32 [64, 256], P(('blk', 'xfer')), may hold values from 0 to 255, as said below
- phase_index: int32 [64, 256], P(('blk', 'xfer')), may hold values from 0 to 7
- partner_slot: int32 [64], P(('blk', 'xfer')), may hold values from 0 to 1, as said below
- conj_index: int32 [256], replicated, may hold values from 0 to 255, as said below
Outputs:
- four_point: float32 [64, 2, 256, 256], P(('blk', 'xfer'))
Inputs may be any that keep to these rules, and one draw needn't show every extreme that they name: `transfer_index`: each row is a permutation: the momentum-frequency shifted by the row's transfer, momenta on a periodic 4 x 4 cluster and frequencies cyclic over 16. `conj_index`: an involution: the index of the negated momentum and the mirrored frequency. `partner_slot`: the pairing is mutual: if transfer q in slot s has partner slot t on the partner device, the transfer in slot t there has partner slot s.
All inputs are finite; a program needn't handle non-finite values.
Results may differ from a plain program's by a relative error of at most 0.0003.
Values may be sent and summed in bfloat16 or wider, within the bound.
No kernel may reach another device: no remote copies, remote signals or barrier semaphores. Data moves between devices by JAX's collectives and lax.ppermute only.
A program may use at most 64 MiB of HBM per device.

v0:
```python
import math
import jax
import jax.numpy as jnp
from jax import lax
from jax.sharding import PartitionSpec as P

NPH = 8


def passed_along(value, axis, by):
    size = lax.axis_size(axis)
    return lax.ppermute(value, axis, [(i, (i + by) % size) for i in range(size)])


def rotations(phase_rows):
    angle = (
        2.0 * math.pi / NPH * (phase_rows[:, :, None] - phase_rows[:, None, :]).astype(jnp.float32)
    )
    return (jnp.cos(angle), jnp.sin(angle))


def selectors(index_rows, width):
    columns = jnp.arange(width, dtype=jnp.int32)
    return (columns[None, :, None] == index_rows[:, None, :]).astype(jnp.bfloat16)


def turned(total, cosines, sines):
    real = cosines * total[:, 0] - sines * total[:, 1]
    imag = cosines * total[:, 1] + sines * total[:, 0]
    return jnp.stack([real, imag], axis=1)


def mirrored(slices, conj_index):
    flipped = jnp.swapaxes(jnp.take(jnp.take(slices, conj_index, axis=2), conj_index, axis=3), 2, 3)
    return jnp.stack([flipped[:, 0], -flipped[:, 1]], axis=1)


def crossed(total, block, index_rows, picking):
    flipped = jnp.swapaxes(block, 1, 2)
    chosen = jnp.take(flipped, index_rows, axis=1)
    moved = jnp.einsum("csaj,sjb->csab", chosen, picking, preferred_element_type=jnp.float32)
    block_real = block[0].astype(jnp.float32)
    block_imag = block[1].astype(jnp.float32)
    real = block_real * moved[0] - block_imag * moved[1]
    imag = block_real * moved[1] + block_imag * moved[0]
    return total + jnp.stack([real, imag], axis=1)


def local(greens, transfer_index, phase_index, partner_slot, conj_index):
    slots = transfer_index.shape[0]
    width = greens.shape[-1]
    blocks = lax.axis_size("blk")
    groups = lax.axis_size("xfer")
    halfway = groups // 2
    scale = 0.5 / math.sqrt(blocks)
    cosines, sines = rotations(phase_index)
    picking = selectors(transfer_index, width)
    empty = jnp.zeros((slots, 2, width, width), jnp.float32)

    def visit(running, block):
        return (crossed(running, block, transfer_index, picking), None)

    sums = lax.scan(visit, empty, lax.all_gather(greens, "blk", axis=0, tiled=True))[0]
    sums = turned(sums, cosines, sines)
    partner = passed_along(sums, "xfer", halfway)
    mirror = jnp.take(partner, partner_slot, axis=0)
    return (sums + mirrored(mirror, conj_index)) * scale


def solution(mesh):
    in_specs = (
        P("blk", None, None, None),
        P(("blk", "xfer"), None),
        P(("blk", "xfer"), None),
        P(("blk", "xfer")),
        P(),
    )
    out_specs = P(("blk", "xfer"), None, None, None)
    return jax.shard_map(local, mesh=mesh, in_specs=in_specs, out_specs=out_specs, check_vma=False)
```

profile of v0, /device:TPU:0, one launch (start us, length us, event | category | flops | bytes accessed | tf_op | source)
XLA Modules:
  0.0 156.7 jit_solution(5556600198563763163)
XLA Ops:
  7.3 32.6 %all-gather.2.cloned.1.call-done = bf16[8,2,256,256]{3,2,1,0:T(8,128)(2,1)} async-done(((bf16[1,2,256,256]{3,2,1,0:T(8,128)(2,1)}), bf16[8,2,256,256]{3,2,1,0:T(8,128)(2,1)}) %all-gather.2.cloned.1.call-update) | async-done | bytes 2097168 | tf_op jit(solution)/shard_map/all_gather | solution.py:63
  39.9 51.2 %while.13 = (s32[]{:T(128)}, f32[2,2,256,256]{3,2,0,1:T(8,128)S(1)}, bf16[8,2,256,256]{3,2,1,0:T(8,128)(2,1)}, s32[2,256]{1,0:T(2,128)}, s32[]{:T(128)}, /*index=5*/s32[]{:T(128)}, s32[]{}) while((s32[]{:T(128)}, f32[2,2,256,256]{3,2,0,1:T(8,128)S(1)}, bf16[8,2,256,256]{3,2,1,0:T(8,128)(2,1)}, ...), condition=%wide.region_1.2_spmd.clone.clone.clone, body=%wide.region_0.1_spmd.clone.clone.clone.sunk | while | flops 136451584 | bytes 11302027 | solution.py:63
  41.8 2.6 %gather_fusion = bf16[512,2,256]{2,1,0:T(2,128)(2,1)S(1)} fusion(bf16[2,256,256]{2,0,1:T(2,128)(2,1)S(1)} %bitcast.71, s32[1024]{0:T(1024)S(1)} %pad_clamp_fusion.4), kind=kCustom, calls=%fused_computation.clone.clone.clone.clone.1 | custom fusion | bytes 1050624 | tf_op jit(solution)/shard_map/while/body/eval_jaxpr/jit(_take)/gather | solution.py:40
  44.8 1.0 fusion.24
  48.2 2.6 %gather_fusion = bf16[512,2,256]{2,1,0:T(2,128)(2,1)S(1)} fusion(bf16[2,256,256]{2,0,1:T(2,128)(2,1)S(1)} %bitcast.71, s32[1024]{0:T(1024)S(1)} %pad_clamp_fusion.4), kind=kCustom, calls=%fused_computation.clone.clone.clone.clone.1 | custom fusion | bytes 1050624 | tf_op jit(solution)/shard_map/while/body/eval_jaxpr/jit(_take)/gather | solution.py:40
  51.2 1.0 fusion.24
  54.6 2.6 %gather_fusion = bf16[512,2,256]{2,1,0:T(2,128)(2,1)S(1)} fusion(bf16[2,256,256]{2,0,1:T(2,128)(2,1)S(1)} %bitcast.71, s32[1024]{0:T(1024)S(1)} %pad_clamp_fusion.4), kind=kCustom, calls=%fused_computation.clone.clone.clone.clone.1 | custom fusion | bytes 1050624 | tf_op jit(solution)/shard_map/while/body/eval_jaxpr/jit(_take)/gather | solution.py:40
  57.6 1.0 fusion.24
  61.0 2.6 %gather_fusion = bf16[512,2,256]{2,1,0:T(2,128)(2,1)S(1)} fusion(bf16[2,256,256]{2,0,1:T(2,128)(2,1)S(1)} %bitcast.71, s32[1024]{0:T(1024)S(1)} %pad_clamp_fusion.4), kind=kCustom, calls=%fused_computation.clone.clone.clone.clone.1 | custom fusion | bytes 1050624 | tf_op jit(solution)/shard_map/while/body/eval_jaxpr/jit(_take)/gather | solution.py:40
  64.0 1.0 fusion.24
  67.4 2.6 %gather_fusion = bf16[512,2,256]{2,1,0:T(2,128)(2,1)S(1)} fusion(bf16[2,256,256]{2,0,1:T(2,128)(2,1)S(1)} %bitcast.71, s32[1024]{0:T(1024)S(1)} %pad_clamp_fusion.4), kind=kCustom, calls=%fused_computation.clone.clone.clone.clone.1 | custom fusion | bytes 1050624 | tf_op jit(solution)/shard_map/while/body/eval_jaxpr/jit(_take)/gather | solution.py:40
  70.4 1.0 fusion.24
  73.8 2.6 %gather_fusion = bf16[512,2,256]{2,1,0:T(2,128)(2,1)S(1)} fusion(bf16[2,256,256]{2,0,1:T(2,128)(2,1)S(1)} %bitcast.71, s32[1024]{0:T(1024)S(1)} %pad_clamp_fusion.4), kind=kCustom, calls=%fused_computation.clone.clone.clone.clone.1 | custom fusion | bytes 1050624 | tf_op jit(solution)/shard_map/while/body/eval_jaxpr/jit(_take)/gather | solution.py:40
  76.8 1.0 fusion.24
  80.2 2.6 %gather_fusion = bf16[512,2,256]{2,1,0:T(2,128)(2,1)S(1)} fusion(bf16[2,256,256]{2,0,1:T(2,128)(2,1)S(1)} %bitcast.71, s32[1024]{0:T(1024)S(1)} %pad_clamp_fusion.4), kind=kCustom, calls=%fused_computation.clone.clone.clone.clone.1 | custom fusion | bytes 1050624 | tf_op jit(solution)/shard_map/while/body/eval_jaxpr/jit(_take)/gather | solution.py:40
  83.2 1.0 fusion.24
  86.6 2.6 %gather_fusion = bf16[512,2,256]{2,1,0:T(2,128)(2,1)S(1)} fusion(bf16[2,256,256]{2,0,1:T(2,128)(2,1)S(1)} %bitcast.71, s32[1024]{0:T(1024)S(1)} %pad_clamp_fusion.4), kind=kCustom, calls=%fused_computation.clone.clone.clone.clone.1 | custom fusion | bytes 1050624 | tf_op jit(solution)/shard_map/while/body/eval_jaxpr/jit(_take)/gather | solution.py:40
  89.6 1.0 fusion.24
  91.2 2.0 %multiply_subtract_fusion.1 = (f32[2,1,256,256]{3,2,1,0:T(8,128)S(1)}, f32[2,1,256,256]{3,2,1,0:T(8,128)S(1)}) fusion(s32[2,256]{1,0:T(2,128)S(1)} %copy-done.1, f32[2,2,256,256]{3,2,0,1:T(8,128)S(1)} %get-tuple-element.32), kind=kLoop, calls=%fused_computation.37 | loop fusion | flops 1179648 | bytes 2101248 | tf_op jit(solution)/shard_map/sub | solution.py:28
  93.3 2.5 %collective-permute-start = (f32[2,2,256,256]{3,2,1,0:T(8,128)S(1)}, f32[2,2,256,256]{3,2,1,0:T(8,128)S(1)}, u32[]{:S(2)}, u32[]{:S(2)}) collective-permute-start(f32[2,2,256,256]{3,2,1,0:T(8,128)S(1)} %pad_maximum_fusion), channel_id=1, source_target_pairs={{0,2},{1,3},{2,0},{3,1},{4,6},{5,7},{6,4},{7,5},{8,10},{9,11},{10,... | collective-permute-start | bytes 3145736 | tf_op jit(solution)/shard_map/ppermute | solution.py:12
  95.9 46.2 %collective-permute-done = f32[2,2,256,256]{3,2,1,0:T(8,128)S(1)} collective-permute-done((f32[2,2,256,256]{3,2,1,0:T(8,128)S(1)}, f32[2,2,256,256]{3,2,1,0:T(8,128)S(1)}, u32[]{:S(2)}, u32[]{:S(2)}) %collective-permute-start) | collective-permute-done | bytes 1048608 | tf_op jit(solution)/shard_map/ppermute | solution.py:12
  143.7 1.9 %gather_fusion.2 = f32[256,2,2,256]{3,2,1,0:T(2,128)S(1)} fusion(f32[2,2,256,256]{3,1,2,0:T(2,128)S(1)} %copy.34, s32[1024]{0:T(1024)S(1)} %pad_clamp_fusion.1), kind=kCustom, calls=%fused_computation.2 | custom fusion | bytes 2098176 | tf_op jit(solution)/shard_map/jit(_take)/gather | solution.py:34
  146.4 1.9 %gather_fusion.3 = f32[256,2,2,256]{3,2,1,0:T(2,128)S(1)} fusion(f32[2,2,256,256]{2,1,3,0:T(2,128)S(1)} %copy.36, s32[1024]{0:T(1024)S(1)} %pad_clamp_fusion.1), kind=kCustom, calls=%fused_computation.3 | custom fusion | bytes 2098176 | tf_op jit(solution)/shard_map/jit(_take)/gather | solution.py:34
  148.7 1.1 fusion.10
  (119 shorter events, 25.5 us)
Async XLA Ops:
  6.5 33.3 %all-gather.2.cloned.1.call-start = ((), (), s32[]{:S(2)}) async-start(), calls=%async_computation | async-start | bytes 2359296 | tf_op jit(solution)/shard_map/all_gather | solution.py:63
  39.9 51.3 %copy-start.1 = (s32[2,256]{1,0:T(2,128)S(1)}, s32[2,256]{1,0:T(2,128)}, u32[]{:S(2)}) copy-start(s32[2,256]{1,0:T(2,128)} %param.9) | copy-start | bytes 6148
  39.9 4.5 %copy-start = (s32[2,256]{1,0:T(2,128)S(1)}, s32[2,256]{1,0:T(2,128)}, u32[]{:S(2)}) copy-start(s32[2,256]{1,0:T(2,128)} %get-tuple-element.146) | copy-start | bytes 6148 | tf_op jit(solution)/shard_map/while
  46.3 4.5 %copy-start = (s32[2,256]{1,0:T(2,128)S(1)}, s32[2,256]{1,0:T(2,128)}, u32[]{:S(2)}) copy-start(s32[2,256]{1,0:T(2,128)} %get-tuple-element.146) | copy-start | bytes 6148 | tf_op jit(solution)/shard_map/while
  52.7 4.5 %copy-start = (s32[2,256]{1,0:T(2,128)S(1)}, s32[2,256]{1,0:T(2,128)}, u32[]{:S(2)}) copy-start(s32[2,256]{1,0:T(2,128)} %get-tuple-element.146) | copy-start | bytes 6148 | tf_op jit(solution)/shard_map/while
  59.1 4.5 %copy-start = (s32[2,256]{1,0:T(2,128)S(1)}, s32[2,256]{1,0:T(2,128)}, u32[]{:S(2)}) copy-start(s32[2,256]{1,0:T(2,128)} %get-tuple-element.146) | copy-start | bytes 6148 | tf_op jit(solution)/shard_map/while
  65.5 4.5 %copy-start = (s32[2,256]{1,0:T(2,128)S(1)}, s32[2,256]{1,0:T(2,128)}, u32[]{:S(2)}) copy-start(s32[2,256]{1,0:T(2,128)} %get-tuple-element.146) | copy-start | bytes 6148 | tf_op jit(solution)/shard_map/while
  71.9 4.5 %copy-start = (s32[2,256]{1,0:T(2,128)S(1)}, s32[2,256]{1,0:T(2,128)}, u32[]{:S(2)}) copy-start(s32[2,256]{1,0:T(2,128)} %get-tuple-element.146) | copy-start | bytes 6148 | tf_op jit(solution)/shard_map/while
  78.3 4.5 %copy-start = (s32[2,256]{1,0:T(2,128)S(1)}, s32[2,256]{1,0:T(2,128)}, u32[]{:S(2)}) copy-start(s32[2,256]{1,0:T(2,128)} %get-tuple-element.146) | copy-start | bytes 6148 | tf_op jit(solution)/shard_map/while
  84.7 4.5 %copy-start = (s32[2,256]{1,0:T(2,128)S(1)}, s32[2,256]{1,0:T(2,128)}, u32[]{:S(2)}) copy-start(s32[2,256]{1,0:T(2,128)} %get-tuple-element.146) | copy-start | bytes 6148 | tf_op jit(solution)/shard_map/while
  91.1 4.7 %copy-start.3 = (s32[2]{0:T(128)S(1)}, s32[2]{0:T(128)}, u32[]{:S(2)}) copy-start(s32[2]{0:T(128)} %param.10) | copy-start | bytes 28
  91.1 4.7 %copy-start.2 = (s32[256]{0:T(256)S(1)}, s32[256]{0:T(256)}, u32[]{:S(2)}) copy-start(s32[256]{0:T(256)} %param.11) | copy-start | bytes 3076
  93.3 48.8 %collective-permute-start = (f32[2,2,256,256]{3,2,1,0:T(8,128)S(1)}, f32[2,2,256,256]{3,2,1,0:T(8,128)S(1)}, u32[]{:S(2)}, u32[]{:S(2)}) collective-permute-start(f32[2,2,256,256]{3,2,1,0:T(8,128)S(1)} %pad_maximum_fusion), channel_id=1, source_target_pairs={{0,2},{1,3},{2,0},{3,1},{4,6},{5,7},{6,4},{7,5},{8,10},{9,11},{10,... | collective-permute-start | bytes 3145736 | tf_op jit(solution)/shard_map/ppermute | solution.py:12
Sparse Core Ops, SparseCore 0:
  9.2 30.5 all-gather.1
where the time goes:
time: 157 us
  waiting for transfers between devices  79.5 us (51%)
  local copies, waits for them, and re-layouts  36.2 us (23%)
  other arithmetic  21.3 us (14%)
  between operations  13.5 us (9%)
  matrix products  2.84 us (2%)
  starting transfers between devices  2.48 us (2%)
    ppermute x1, waiting for transfers between devices, passed_along(): lax.ppermute(value, axis, [(i, (i + by) % size) for i in range(size)])  46.2 us
    all_gather x1, waiting for transfers between devices, local(): lax.all_gather(greens, 'blk', axis=0, tiled=True)  32.6 us
    gather x16, local copies, waits for them, and re-layouts, crossed(): chosen = jnp.take(flipped, index_rows, axis=1)  21.1 us
    dynamic_slice x16, local copies, waits for them, and re-layouts, local(): lax.scan(visit, empty, lax.all_gather(greens, 'blk', axis=0, tiled=True))[0]  9.24 us
    convert_element_type x8, other arithmetic, crossed(): block_real = block[0].astype(jnp.float32)  8.09 us
    while x8, other arithmetic  5.49 us
  transfers between devices with their start and end apart: 2, of which 2 were waited for; matrix products, arithmetic and copies ran while one was open for 0% of the time, Pallas kernels for 0%

commit v1 on v0

--- a/solution.py
+++ b/solution.py
@@ -5,6 +5,24 @@
 from jax.sharding import PartitionSpec as P
 
 NPH = 8
+
+
+def ring_gather(value, axis, dim):
+    ways, here, turn = (lax.axis_size(axis), lax.axis_index(axis), value.shape[dim])
+    shape = [n * ways if d == dim else n for d, n in enumerate(value.shape)]
+    full = lax.dynamic_update_slice_in_dim(
+        jnp.zeros(shape, value.dtype), value, here * turn, axis=dim
+    )
+    going_up = going_down = value
+    for far in range(1, ways // 2 + 1):
+        going_up = lax.ppermute(going_up, axis, [(d, (d + 1) % ways) for d in range(ways)])
+        full = lax.dynamic_update_slice_in_dim(full, going_up, (here - far) % ways * turn, axis=dim)
+        if 2 * far < ways:
+            going_down = lax.ppermute(going_down, axis, [(d, (d - 1) % ways) for d in range(ways)])
+            full = lax.dynamic_update_slice_in_dim(
+                full, going_down, (here + far) % ways * turn, axis=dim
+            )
+    return full
 
 
 def passed_along(value, axis, by):
@@ -60,7 +78,7 @@
     def visit(running, block):
         return (crossed(running, block, transfer_index, picking), None)
 
-    sums = lax.scan(visit, empty, lax.all_gather(greens, "blk", axis=0, tiled=True))[0]
+    sums = lax.scan(visit, empty, ring_gather(greens, "blk", 0))[0]
     sums = turned(sums, cosines, sines)
     partner = passed_along(sums, "xfer", halfway)
     mirror = jnp.take(partner, partner_slot, axis=0)

time: 157 us -> 134 us (0.85)
  waiting for transfers between devices: 79.5 us -> 53.8 us
  starting transfers between devices: 2.48 us -> 16.8 us
  between operations: 13.5 us -> 0.17 us
  local copies, waits for them, and re-layouts: 36.2 us -> 43.4 us
  other arithmetic: 21.3 us -> 15.8 us
    all_gather x1 -> x0, waiting for transfers between devices: 32.6 us -> none  [local(): lax.all_gather(greens, 'blk', axis=0, tiled=True)]
    ppermute x0 -> x7, waiting for transfers between devices: none -> 12.2 us  [the longest x4 10.4 us: ring_gather(): lax.ppermute(going_up, axis, [(d, (d + 1) % ways) for d in range(ways)])]
    ppermute x0 -> x7, starting transfers between devices: none -> 9.56 us  [the longest x3 8.44 us: ring_gather(): lax.ppermute(going_down, axis, [(d, (d - 1) % ways) for d in range(ways)])]
    dynamic_update_slice x0 -> x8, local copies, waits for them, and re-layouts: none -> 5.78 us  [the longest x4 2.92 us: ring_gather(): lax.dynamic_update_slice_in_dim(full, going_up, (here - far) % ways * tur...]
    while x8, other arithmetic: 5.49 us -> 0.03 us
    ppermute x1, starting transfers between devices: 2.48 us -> 7.21 us  [passed_along(): lax.ppermute(value, axis, [(i, (i + by) % size) for i in range(size)])]
    ppermute x1, waiting for transfers between devices: 46.2 us -> 41.7 us  [passed_along(): lax.ppermute(value, axis, [(i, (i + by) % size) for i in range(size)])]
  transfers between devices with their start and end apart: 2 -> 8, of which waited for: 2 -> 8; matrix products, arithmetic and copies ran while one was open for 0% -> 5% of each run, Pallas kernels for 0% -> 0%
where the time goes in v1:
time: 134 us
  waiting for transfers between devices  53.8 us (40%)
  local copies, waits for them, and re-layouts  43.4 us (32%)
  starting transfers between devices  16.8 us (13%)
  other arithmetic  15.8 us (12%)
  matrix products  2.84 us (2%)
    ppermute x1, waiting for transfers between devices, passed_along(): lax.ppermute(value, axis, [(i, (i + by) % size) for i in range(size)])  41.7 us
    gather x16, local copies, waits for them, and re-layouts, crossed(): chosen = jnp.take(flipped, index_rows, axis=1)  21.1 us
    ppermute x4, waiting for transfers between devices, ring_gather(): lax.ppermute(going_up, axis, [(d, (d + 1) % ways) for d in range(ways)])  10.4 us
    dynamic_slice x16, local copies, waits for them, and re-layouts, local(): sums = lax.scan(visit, empty, ring_gather(greens, 'blk', 0))[0]  9.21 us
    ppermute x3, starting transfers between devices, ring_gather(): lax.ppermute(going_down, axis, [(d, (d - 1) % ways) for d in range(ways)])  8.44 us
    convert_element_type x8, other arithmetic, crossed(): block_real = block[0].astype(jnp.float32)  8.09 us
    ppermute x1, starting transfers between devices, passed_along(): lax.ppermute(value, axis, [(i, (i + by) % size) for i in range(size)])  7.21 us
    dynamic_update_slice x4, local copies, waits for them, and re-layouts, ring_gather(): lax.dynamic_update_slice_in_dim(full, going_up, (here - far) % ways * tur...  2.92 us
  transfers between devices with their start and end apart: 8, of which 8 were waited for; matrix products, arithmetic and copies ran while one was open for 5% of the time, Pallas kernels for 0%

profile of v1, /device:TPU:0, one launch (start us, length us, event | category | flops | bytes accessed | tf_op | source)
XLA Modules:
  0.0 133.7 jit_solution(9105344702761095299)
XLA Ops:
  0.5 2.9 %collective-permute-start.1 = (bf16[1,2,256,256]{3,2,1,0:T(8,128)(2,1)}, bf16[1,2,256,256]{3,2,1,0:T(8,128)(2,1)S(1)}, u32[]{:S(2)}, u32[]{:S(2)}) collective-permute-start(bf16[1,2,256,256]{3,2,1,0:T(8,128)(2,1)} %param.7), channel_id=1, source_target_pairs={{0,28},{4,0},{8,4},{12,8},{16,12},{20,16},{24,20},{28,24},{1,29},{... | collective-permute-start | bytes 786440 | tf_op jit(solution)/shard_map/ppermute | solution.py:21
  3.4 4.5 %collective-permute-done = bf16[1,2,256,256]{3,2,1,0:T(8,128)(2,1)S(1)} collective-permute-done((bf16[1,2,256,256]{3,2,1,0:T(8,128)(2,1)}, bf16[1,2,256,256]{3,2,1,0:T(8,128)(2,1)S(1)}, u32[]{:S(2)}, u32[]{:S(2)}) %collective-permute-start) | collective-permute-done | bytes 262176 | tf_op jit(solution)/shard_map/ppermute | solution.py:18
  9.4 2.7 %collective-permute-start.3 = (bf16[1,2,256,256]{3,2,1,0:T(8,128)(2,1)S(1)}, bf16[1,2,256,256]{3,2,1,0:T(8,128)(2,1)S(1)}, u32[]{:S(2)}, u32[]{:S(2)}) collective-permute-start(bf16[1,2,256,256]{3,2,1,0:T(8,128)(2,1)S(1)} %collective-permute-done.1), channel_id=1, source_target_pairs={{0,28},{4,0},{8,4},{12,8},{16,12},{20,16},{24,20},{28,24},{1,29},{... | collective-permute-start | bytes 786440 | tf_op jit(solution)/shard_map/ppermute | solution.py:21
  12.1 1.5 %broadcast_in_dim.55 = bf16[8,2,256,256]{3,2,1,0:T(8,128)(2,1)} broadcast(bf16[]{:T(256)} %constant.112.clone.1), dimensions={} | broadcast | bytes 2097154 | tf_op jit(solution)/shard_map/broadcast_in_dim | solution.py:14
  16.9 2.8 %collective-permute-start.5 = (bf16[1,2,256,256]{3,2,1,0:T(8,128)(2,1)S(1)}, bf16[1,2,256,256]{3,2,1,0:T(8,128)(2,1)S(1)}, u32[]{:S(2)}, u32[]{:S(2)}) collective-permute-start(bf16[1,2,256,256]{3,2,1,0:T(8,128)(2,1)S(1)} %collective-permute-done.3), channel_id=1, source_target_pairs={{0,28},{4,0},{8,4},{12,8},{16,12},{20,16},{24,20},{28,24},{1,29},{... | collective-permute-start | bytes 786440 | tf_op jit(solution)/shard_map/ppermute | solution.py:21
  20.4 1.3 collective-permute-done.4
  24.3 4.1 %collective-permute-done.6 = bf16[1,2,256,256]{3,2,1,0:T(8,128)(2,1)S(1)} collective-permute-done((bf16[1,2,256,256]{3,2,1,0:T(8,128)(2,1)S(1)}, bf16[1,2,256,256]{3,2,1,0:T(8,128)(2,1)S(1)}, u32[]{:S(2)}, u32[]{:S(2)}) %collective-permute-start.6) | collective-permute-done | bytes 262176 | tf_op jit(solution)/shard_map/ppermute | solution.py:18
  29.1 45.7 %while.13 = (s32[]{:T(128)}, f32[2,2,256,256]{3,2,0,1:T(8,128)S(1)}, bf16[8,2,256,256]{3,2,1,0:T(8,128)(2,1)}, s32[2,256]{1,0:T(2,128)S(1)}, s32[]{:T(128)}, /*index=5*/s32[]{:T(128)}, s32[]{}) while((s32[]{:T(128)}, f32[2,2,256,256]{3,2,0,1:T(8,128)S(1)}, bf16[8,2,256,256]{3,2,1,0:T(8,128)(2,1)}, ...), condition=%wide.region_1.2_spmd.clone.clone.clone, body=%wide.region_0.1_spmd.clone.clone.clone.sunk | while | flops 136451584 | bytes 11293807 | solution.py:81
  30.3 2.6 %gather_fusion = bf16[512,2,256]{2,1,0:T(2,128)(2,1)S(1)} fusion(bf16[2,256,256]{2,0,1:T(2,128)(2,1)S(1)} %bitcast.71, s32[1024]{0:T(1024)S(1)} %pad_clamp_fusion.4), kind=kCustom, calls=%fused_computation.clone.clone.clone.clone.1 | custom fusion | bytes 1050624 | tf_op jit(solution)/shard_map/while/body/eval_jaxpr/jit(_take)/gather | solution.py:58
  33.3 1.0 fusion.24
  36.0 2.6 %gather_fusion = bf16[512,2,256]{2,1,0:T(2,128)(2,1)S(1)} fusion(bf16[2,256,256]{2,0,1:T(2,128)(2,1)S(1)} %bitcast.71, s32[1024]{0:T(1024)S(1)} %pad_clamp_fusion.4), kind=kCustom, calls=%fused_computation.clone.clone.clone.clone.1 | custom fusion | bytes 1050624 | tf_op jit(solution)/shard_map/while/body/eval_jaxpr/jit(_take)/gather | solution.py:58
  39.1 1.0 fusion.24
  41.7 2.6 %gather_fusion = bf16[512,2,256]{2,1,0:T(2,128)(2,1)S(1)} fusion(bf16[2,256,256]{2,0,1:T(2,128)(2,1)S(1)} %bitcast.71, s32[1024]{0:T(1024)S(1)} %pad_clamp_fusion.4), kind=kCustom, calls=%fused_computation.clone.clone.clone.clone.1 | custom fusion | bytes 1050624 | tf_op jit(solution)/shard_map/while/body/eval_jaxpr/jit(_take)/gather | solution.py:58
  47.5 2.6 %gather_fusion = bf16[512,2,256]{2,1,0:T(2,128)(2,1)S(1)} fusion(bf16[2,256,256]{2,0,1:T(2,128)(2,1)S(1)} %bitcast.71, s32[1024]{0:T(1024)S(1)} %pad_clamp_fusion.4), kind=kCustom, calls=%fused_computation.clone.clone.clone.clone.1 | custom fusion | bytes 1050624 | tf_op jit(solution)/shard_map/while/body/eval_jaxpr/jit(_take)/gather | solution.py:58
  53.2 2.6 %gather_fusion = bf16[512,2,256]{2,1,0:T(2,128)(2,1)S(1)} fusion(bf16[2,256,256]{2,0,1:T(2,128)(2,1)S(1)} %bitcast.71, s32[1024]{0:T(1024)S(1)} %pad_clamp_fusion.4), kind=kCustom, calls=%fused_computation.clone.clone.clone.clone.1 | custom fusion | bytes 1050624 | tf_op jit(solution)/shard_map/while/body/eval_jaxpr/jit(_take)/gather | solution.py:58
  58.9 2.6 %gather_fusion = bf16[512,2,256]{2,1,0:T(2,128)(2,1)S(1)} fusion(bf16[2,256,256]{2,0,1:T(2,128)(2,1)S(1)} %bitcast.71, s32[1024]{0:T(1024)S(1)} %pad_clamp_fusion.4), kind=kCustom, calls=%fused_computation.clone.clone.clone.clone.1 | custom fusion | bytes 1050624 | tf_op jit(solution)/shard_map/while/body/eval_jaxpr/jit(_take)/gather | solution.py:58
  64.6 2.6 %gather_fusion = bf16[512,2,256]{2,1,0:T(2,128)(2,1)S(1)} fusion(bf16[2,256,256]{2,0,1:T(2,128)(2,1)S(1)} %bitcast.71, s32[1024]{0:T(1024)S(1)} %pad_clamp_fusion.4), kind=kCustom, calls=%fused_computation.clone.clone.clone.clone.1 | custom fusion | bytes 1050624 | tf_op jit(solution)/shard_map/while/body/eval_jaxpr/jit(_take)/gather | solution.py:58
  70.3 2.6 %gather_fusion = bf16[512,2,256]{2,1,0:T(2,128)(2,1)S(1)} fusion(bf16[2,256,256]{2,0,1:T(2,128)(2,1)S(1)} %bitcast.71, s32[1024]{0:T(1024)S(1)} %pad_clamp_fusion.4), kind=kCustom, calls=%fused_computation.clone.clone.clone.clone.1 | custom fusion | bytes 1050624 | tf_op jit(solution)/shard_map/while/body/eval_jaxpr/jit(_take)/gather | solution.py:58
  74.9 2.0 %multiply_subtract_fusion.1 = (f32[2,1,256,256]{3,2,1,0:T(8,128)S(1)}, f32[2,1,256,256]{3,2,1,0:T(8,128)S(1)}) fusion(s32[2,256]{1,0:T(2,128)S(1)} %copy-done.2, f32[2,2,256,256]{3,2,0,1:T(8,128)S(1)} %get-tuple-element.32), kind=kLoop, calls=%fused_computation.37 | loop fusion | flops 1179648 | bytes 2101248 | tf_op jit(solution)/shard_map/sub | solution.py:46
  77.0 7.2 %collective-permute-start.7 = (f32[2,2,256,256]{3,2,1,0:T(8,128)S(1)}, f32[2,2,256,256]{3,2,1,0:T(8,128)S(1)}, u32[]{:S(2)}, u32[]{:S(2)}) collective-permute-start(f32[2,2,256,256]{3,2,1,0:T(8,128)S(1)} %pad_maximum_fusion), channel_id=1, source_target_pairs={{0,2},{1,3},{2,0},{3,1},{4,6},{5,7},{6,4},{7,5},{8,10},{9,11},{10,... | collective-permute-start | bytes 3145736 | tf_op jit(solution)/shard_map/ppermute | solution.py:30
  84.3 41.7 %collective-permute-done.7 = f32[2,2,256,256]{3,2,1,0:T(8,128)S(1)} collective-permute-done((f32[2,2,256,256]{3,2,1,0:T(8,128)S(1)}, f32[2,2,256,256]{3,2,1,0:T(8,128)S(1)}, u32[]{:S(2)}, u32[]{:S(2)}) %collective-permute-start.7) | collective-permute-done | bytes 1048608 | tf_op jit(solution)/shard_map/ppermute | solution.py:30
  127.6 1.9 %gather_fusion.2 = f32[256,2,2,256]{3,2,1,0:T(2,128)S(1)} fusion(f32[2,2,256,256]{3,1,2,0:T(2,128)S(1)} %copy.25, s32[1024]{0:T(1024)S(1)} %pad_clamp_fusion.1), kind=kCustom, calls=%fused_computation.2 | custom fusion | bytes 2098176 | tf_op jit(solution)/shard_map/jit(_take)/gather | solution.py:52
  130.3 1.9 %gather_fusion.3 = f32[256,2,2,256]{3,2,1,0:T(2,128)S(1)} fusion(f32[2,2,256,256]{2,1,3,0:T(2,128)S(1)} %copy.27, s32[1024]{0:T(1024)S(1)} %pad_clamp_fusion.1), kind=kCustom, calls=%fused_computation.3 | custom fusion | bytes 2098176 | tf_op jit(solution)/shard_map/jit(_take)/gather | solution.py:52
  132.6 1.1 fusion.10
  (127 shorter events, 34.6 us)
Async XLA Ops:
  0.0 13.6 %copy-start = (bf16[1,2,256,256]{3,2,1,0:T(8,128)(2,1)S(1)}, bf16[1,2,256,256]{3,2,1,0:T(8,128)(2,1)}, u32[]{:S(2)}) copy-start(bf16[1,2,256,256]{3,2,1,0:T(8,128)(2,1)} %param.7) | copy-start | bytes 786436
  0.0 7.9 %collective-permute-start = (bf16[1,2,256,256]{3,2,1,0:T(8,128)(2,1)}, bf16[1,2,256,256]{3,2,1,0:T(8,128)(2,1)S(1)}, u32[]{:S(2)}, u32[]{:S(2)}) collective-permute-start(bf16[1,2,256,256]{3,2,1,0:T(8,128)(2,1)} %param.7), channel_id=1, source_target_pairs={{0,4},{4,8},{8,12},{12,16},{16,20},{20,24},{24,28},{28,0},{1,5},{5... | collective-permute-start | bytes 786440 | tf_op jit(solution)/shard_map/ppermute | solution.py:18
  0.5 8.9 %collective-permute-start.1 = (bf16[1,2,256,256]{3,2,1,0:T(8,128)(2,1)}, bf16[1,2,256,256]{3,2,1,0:T(8,128)(2,1)S(1)}, u32[]{:S(2)}, u32[]{:S(2)}) collective-permute-start(bf16[1,2,256,256]{3,2,1,0:T(8,128)(2,1)} %param.7), channel_id=1, source_target_pairs={{0,28},{4,0},{8,4},{12,8},{16,12},{20,16},{24,20},{28,24},{1,29},{... | collective-permute-start | bytes 786440 | tf_op jit(solution)/shard_map/ppermute | solution.py:21
  7.9 7.0 %collective-permute-start.2 = (bf16[1,2,256,256]{3,2,1,0:T(8,128)(2,1)S(1)}, bf16[1,2,256,256]{3,2,1,0:T(8,128)(2,1)S(1)}, u32[]{:S(2)}, u32[]{:S(2)}) collective-permute-start(bf16[1,2,256,256]{3,2,1,0:T(8,128)(2,1)S(1)} %collective-permute-done), channel_id=1, source_target_pairs={{0,4},{4,8},{8,12},{12,16},{16,20},{20,24},{24,28},{28,0},{1,5},{5... | collective-permute-start | bytes 786440 | tf_op jit(solution)/shard_map/ppermute | solution.py:18
  9.4 7.5 %collective-permute-start.3 = (bf16[1,2,256,256]{3,2,1,0:T(8,128)(2,1)S(1)}, bf16[1,2,256,256]{3,2,1,0:T(8,128)(2,1)S(1)}, u32[]{:S(2)}, u32[]{:S(2)}) collective-permute-start(bf16[1,2,256,256]{3,2,1,0:T(8,128)(2,1)S(1)} %collective-permute-done.1), channel_id=1, source_target_pairs={{0,28},{4,0},{8,4},{12,8},{16,12},{20,16},{24,20},{28,24},{1,29},{... | collective-permute-start | bytes 786440 | tf_op jit(solution)/shard_map/ppermute | solution.py:21
  13.6 15.5 %copy-start.1 = (s32[2,256]{1,0:T(2,128)S(1)}, s32[2,256]{1,0:T(2,128)}, u32[]{:S(2)}) copy-start(s32[2,256]{1,0:T(2,128)} %param.8) | copy-start | bytes 6148
  14.9 6.8 %collective-permute-start.4 = (bf16[1,2,256,256]{3,2,1,0:T(8,128)(2,1)S(1)}, bf16[1,2,256,256]{3,2,1,0:T(8,128)(2,1)S(1)}, u32[]{:S(2)}, u32[]{:S(2)}) collective-permute-start(bf16[1,2,256,256]{3,2,1,0:T(8,128)(2,1)S(1)} %collective-permute-done.2), channel_id=1, source_target_pairs={{0,4},{4,8},{8,12},{12,16},{16,20},{20,24},{24,28},{28,0},{1,5},{5... | collective-permute-start | bytes 786440 | tf_op jit(solution)/shard_map/ppermute | solution.py:18
  16.9 6.7 %collective-permute-start.5 = (bf16[1,2,256,256]{3,2,1,0:T(8,128)(2,1)S(1)}, bf16[1,2,256,256]{3,2,1,0:T(8,128)(2,1)S(1)}, u32[]{:S(2)}, u32[]{:S(2)}) collective-permute-start(bf16[1,2,256,256]{3,2,1,0:T(8,128)(2,1)S(1)} %collective-permute-done.3), channel_id=1, source_target_pairs={{0,28},{4,0},{8,4},{12,8},{16,12},{20,16},{24,20},{28,24},{1,29},{... | collective-permute-start | bytes 786440 | tf_op jit(solution)/shard_map/ppermute | solution.py:21
  21.7 6.7 %collective-permute-start.6 = (bf16[1,2,256,256]{3,2,1,0:T(8,128)(2,1)S(1)}, bf16[1,2,256,256]{3,2,1,0:T(8,128)(2,1)S(1)}, u32[]{:S(2)}, u32[]{:S(2)}) collective-permute-start(bf16[1,2,256,256]{3,2,1,0:T(8,128)(2,1)S(1)} %collective-permute-done.4), channel_id=1, source_target_pairs={{0,4},{4,8},{8,12},{12,16},{16,20},{20,24},{24,28},{28,0},{1,5},{5... | collective-permute-start | bytes 786440 | tf_op jit(solution)/shard_map/ppermute | solution.py:18
  29.1 45.8 %copy-start.2 = (s32[2,256]{1,0:T(2,128)S(1)}, s32[2,256]{1,0:T(2,128)}, u32[]{:S(2)}) copy-start(s32[2,256]{1,0:T(2,128)} %param.9) | copy-start | bytes 6148
  74.9 9.4 %copy-start.4 = (s32[2]{0:T(128)S(1)}, s32[2]{0:T(128)}, u32[]{:S(2)}) copy-start(s32[2]{0:T(128)} %param.10) | copy-start | bytes 28
  74.9 9.4 %copy-start.3 = (s32[256]{0:T(256)S(1)}, s32[256]{0:T(256)}, u32[]{:S(2)}) copy-start(s32[256]{0:T(256)} %param.11) | copy-start | bytes 3076
  77.0 49.0 %collective-permute-start.7 = (f32[2,2,256,256]{3,2,1,0:T(8,128)S(1)}, f32[2,2,256,256]{3,2,1,0:T(8,128)S(1)}, u32[]{:S(2)}, u32[]{:S(2)}) collective-permute-start(f32[2,2,256,256]{3,2,1,0:T(8,128)S(1)} %pad_maximum_fusion), channel_id=1, source_target_pairs={{0,2},{1,3},{2,0},{3,1},{4,6},{5,7},{6,4},{7,5},{8,10},{9,11},{10,... | collective-permute-start | bytes 3145736 | tf_op jit(solution)/shard_map/ppermute | solution.py:30
